TPU v7x, 32 devices: a whole 2x2x4 slice. The times are simulated.
32 devices in a mesh: gx: 8 (over y, x, core), gy: 4 (over z).
Axes of the slice: x: 2, y: 2, z: 4, core: 2. Of those that a mesh axis runs over, the one named last changes fastest.
Arguments:
- temp_start: float32 [8, 1024, 2048], P(None, ('gx', 'gy')), may hold values from -6 to 6
- heat_input: float32 [8, 1024, 2048], P(None, ('gx', 'gy')), may hold values from -3 to 3
- lateral: float32 [8], replicated, may hold values from 0.03 to 0.15
- vertical: float32 [7], replicated, may hold values from 0.03 to 0.15
- weighting: float32 [8], replicated, may hold values from -1 to 1
- modulus: float32 [1024, 2048], P('gx', 'gy'), may hold values from 0.3 to 3
- warp_prev: float32 [1024, 2048], P('gx', 'gy'), may hold values from -6 to 6
- joint_cell: int32 [65536], P(('gx', 'gy')), may hold values from 0 to 65535
- joint_owner: int32 [65536, 1], P(('gx', 'gy')), may hold values from 0 to 31; in each aligned block of 2048 rows (0 to 2047, 2048 to 4095, ...) at most 192 rows name the same one
- joint_strain: float32 [2, 32, 6144], P(None, ('gx', 'gy')), may hold values from -4 to 4
- joint_resist: float32 [32, 6144], P(('gx', 'gy')), may hold values from 1 to 2
Outputs:
- warpage: float32 [1024, 2048], P('gx', 'gy')
- strain_next: float32 [2, 32, 6144], P(None, ('gx', 'gy'))
- resist_next: float32 [32, 6144], P(('gx', 'gy'))
Inputs may be any that keep to these rules, and one draw needn't show every extreme that they name: `joint_owner`: among the 2048 joints of one device at most 192 have the same owner, and on some device exactly 192 do.
All inputs are finite; a program needn't handle non-finite values.
Results may differ from a plain program's by a relative error of at most 0.0003.
Values sent between devices are 32-bit elements; how exact they have to be, the bound alone decides.
No kernel may reach another device: no remote copies, remote signals or barrier semaphores. Data moves between devices by JAX's collectives and lax.ppermute only.
A program may use at most 320 MiB of HBM per device.

v0:
```python
import jax
import jax.numpy as jnp
from jax import lax
from jax.sharding import PartitionSpec as P

STEPS = 2
SWEEPS = 3
stiffness = 0.2
shear_mod = 0.6
rate_scale = 0.5
sat_level = 2.5
sat_power = 0.3
harden = 2.0


def with_halo(array, sides, width):
    for axis, dim in sides:
        count, length = (lax.axis_size(axis), array.shape[dim])
        up = [(i, (i + 1) % count) for i in range(count - 1)]
        down = [(j, i) for i, j in up]
        last = lax.slice_in_dim(array, length - width, length, axis=dim)
        leading = lax.slice_in_dim(array, 0, width, axis=dim)
        before = lax.ppermute(last, axis, up)
        after = lax.ppermute(leading, axis, down)
        array = jnp.concatenate([before, array, after], axis=dim)
    return array


def thermal_step(ext, heat_rows, lateral, vertical):
    cols = jnp.pad(ext, ((0, 0), (0, 0), (1, 1)))
    center = ext[:, 1:-1]
    lap = ext[:, 2:] + ext[:, :-2] + cols[:, 1:-1, 2:] + cols[:, 1:-1, :-2] - 4.0 * center
    flux = vertical[:, None, None] * (center[1:] - center[:-1])
    vert = jnp.pad(flux, ((0, 1), (0, 0), (0, 0))) - jnp.pad(flux, ((1, 0), (0, 0), (0, 0)))
    return center + lateral[:, None, None] * lap + vert + heat_rows


def moment_of(field, weighting):
    total = weighting[0] * field[0]
    for layer in range(1, field.shape[0]):
        total = total + weighting[layer] * field[layer]
    return total


def sweep(w_pad, e_pad, load):
    center = e_pad[1:-1, 1:-1]
    e_up = 0.5 * (center + e_pad[:-2, 1:-1])
    e_down = 0.5 * (center + e_pad[2:, 1:-1])
    e_left = 0.5 * (center + e_pad[1:-1, :-2])
    e_right = 0.5 * (center + e_pad[1:-1, 2:])
    numer = (
        load
        + e_up * w_pad[:-2, 1:-1]
        + e_down * w_pad[2:, 1:-1]
        + e_left * w_pad[1:-1, :-2]
        + e_right * w_pad[1:-1, 2:]
    )
    denom = stiffness + e_up + e_down + e_left + e_right
    return numer / denom


def anand(strain, resist, recv):
    total, inelastic = (strain[0], strain[1])
    increment, theta, live = (recv[0], recv[1], recv[2])
    total_new = total + increment
    arrhen = jnp.exp(2.0 - 2.0 / (1.0 + 0.1 * theta * theta))
    hyper = jnp.sinh(shear_mod * (total_new - inelastic) / resist)
    rate = rate_scale * arrhen * hyper * jnp.abs(hyper)
    inelastic_new = inelastic + rate
    target = sat_level * jnp.power(1.0 + jnp.abs(rate) / arrhen, sat_power)
    resist_new = resist + harden * (1.0 - resist / target) * jnp.abs(rate)
    keep = live > 0.5
    strain_out = jnp.stack(
        [jnp.where(keep, total_new, total), jnp.where(keep, inelastic_new, inelastic)]
    )
    return (strain_out, jnp.where(keep, resist_new, resist))


def body(
    temp_start,
    heat_input,
    lateral,
    vertical,
    weighting,
    modulus,
    warp_prev,
    joint_cell,
    joint_owner,
    joint_strain,
    joint_resist,
):
    devices = lax.axis_size(("gx", "gy"))
    temp = temp_start
    for step in range(STEPS):
        ext = with_halo(temp, ((("gx", "gy"), 1),), 1)
        temp = thermal_step(ext, heat_input, lateral, vertical)
    relayed = lax.all_to_all(temp, "gy", split_axis=2, concat_axis=1, tiled=True)
    load = moment_of(relayed, weighting)
    top = relayed[-1]
    e_pad = with_halo(modulus, (("gx", 0), ("gy", 1)), 1)
    warp = warp_prev
    for step in range(SWEEPS):
        w_pad = with_halo(warp, (("gx", 0), ("gy", 1)), 1)
        warp = sweep(w_pad, e_pad, load)
    capacity = joint_resist.shape[1] // devices
    owners = joint_owner[:, 0]
    increment = warp.reshape(-1)[joint_cell] - warp_prev.reshape(-1)[joint_cell]
    theta = top.reshape(-1)[joint_cell]
    values = jnp.stack([increment, theta, jnp.ones_like(theta)])
    onehot = (owners[:, None] == jnp.arange(devices, dtype=jnp.int32)[None, :]).astype(jnp.int32)
    ranks = jnp.sum(jnp.cumsum(onehot, axis=0) * onehot, axis=1) - 1
    slots = owners * capacity + ranks
    outgoing = jnp.zeros((3, devices * capacity), jnp.float32).at[:, slots].set(values)
    incoming = lax.all_to_all(outgoing, ("gx", "gy"), split_axis=1, concat_axis=1, tiled=True)
    strain_next, resist_next = anand(joint_strain, joint_resist, incoming[:, None, :])
    return (warp, strain_next, resist_next)


def solution(mesh):
    return jax.shard_map(
        body,
        mesh=mesh,
        in_specs=(
            P(None, ("gx", "gy"), None),
            P(None, ("gx", "gy"), None),
            P(),
            P(),
            P(),
            P("gx", "gy"),
            P("gx", "gy"),
            P(("gx", "gy")),
            P(("gx", "gy"), None),
            P(None, ("gx", "gy"), None),
            P(("gx", "gy"), None),
        ),
        out_specs=(P("gx", "gy"), P(None, ("gx", "gy"), None), P(("gx", "gy"), None)),
        check_vma=False,
    )
```

profile of v0, /device:TPU:0, one launch (start us, length us, event | category | flops | bytes accessed | tf_op | source)
XLA Modules:
  0.0 217.0 jit_solution(10733385116861195216)
XLA Ops:
  4.8 5.6 %collective-permute-start.1 = (f32[8,1,2048]{2,0,1:T(8,128)S(1)}, f32[8,1,2048]{2,0,1:T(8,128)S(1)}, u32[]{:S(2)}, u32[]{:S(2)}) collective-permute-start(f32[8,1,2048]{2,0,1:T(8,128)S(1)} %get-tuple-element.11), channel_id=1, source_target_pairs={{0,1},{1,2},{2,3},{3,4},{4,5},{5,6},{6,7},{7,8},{8,9},{9,10},{10,1... | collective-permute-start | bytes 196616 | tf_op jit(solution)/shard_map/ppermute | solution.py:23
  17.0 5.0 %collective-permute-start.3 = (f32[8,1,2048]{2,0,1:T(8,128)S(1)}, f32[8,1,2048]{2,0,1:T(8,128)S(1)}, u32[]{:S(2)}, u32[]{:S(2)}) collective-permute-start(f32[8,1,2048]{2,0,1:T(8,128)S(1)} %get-tuple-element.9), channel_id=1, source_target_pairs={{0,1},{1,2},{2,3},{3,4},{4,5},{5,6},{6,7},{7,8},{8,9},{9,10},{10,1... | collective-permute-start | bytes 196616 | tf_op jit(solution)/shard_map/ppermute | solution.py:23
  27.2 4.9 %copy.63 = f32[8,32,2048]{1,0,2:T(8,128)} copy(f32[8,32,2048]{2,0,1:T(8,128)S(1)} %fusion.6) | data formatting | bytes 4194304 | tf_op jit(solution)/shard_map/add | solution.py:35
  32.1 7.1 %reshape.264 = f32[4,1,131072]{2,1,0:T(1,128)} reshape(f32[2048,8,32]{2,1,0:T(8,128)} %bitcast.70) | data formatting | bytes 4194304
  39.2 8.6 %all-to-all-start = ((f32[4,1,131072]{2,1,0:T(1,128)}), f32[4,1,131072]{2,1,0:T(1,128)S(1)}, u32[]{:S(2)}, u32[]{:S(2)}) async-start(f32[4,1,131072]{2,1,0:T(1,128)} %reshape.264), calls=%async_computation | async-start | bytes 4194304 | tf_op jit(solution)/shard_map/all_to_all | solution.py:97
  47.8 4.4 %collective-permute-start.4 = (f32[1,512]{1,0:T(1,128)S(1)}, f32[1,512]{1,0:T(1,128)S(1)}, u32[]{:S(2)}, u32[]{:S(2)}) collective-permute-start(f32[1,512]{1,0:T(1,128)S(1)} %get-tuple-element.26), channel_id=1, source_target_pairs={{0,4},{4,8},{8,12},{12,16},{16,20},{20,24},{24,28},{1,5},{5,9},{9,... | collective-permute-start | bytes 6152 | tf_op jit(solution)/shard_map/ppermute | solution.py:23
  53.6 5.2 %collective-permute-start.5 = (f32[1,512]{1,0:T(1,128)S(1)}, f32[1,512]{1,0:T(1,128)S(1)}, u32[]{:S(2)}, u32[]{:S(2)}) collective-permute-start(f32[1,512]{1,0:T(1,128)S(1)} %get-tuple-element.27), channel_id=1, source_target_pairs={{0,4},{4,8},{8,12},{12,16},{16,20},{20,24},{24,28},{1,5},{5,9},{9,... | collective-permute-start | bytes 6152 | tf_op jit(solution)/shard_map/ppermute | solution.py:23
  60.2 9.1 %reduce-window.6 = s32[32,16,128]{2,1,0:T(8,128)S(1)} reduce-window(s32[32,16,128]{2,1,0:T(8,128)S(1)} %fusion.61, s32[]{:T(128)} %constant.6.clone.1), window={size=1x1x128 pad=0_0x0_0x127_0}, to_apply=%region_0.1 | reduce-window | flops 8323072 | bytes 524292 | tf_op jit(solution)/shard_map/reduce-window
  72.2 4.5 %collective-permute-start.8 = (f32[130,1]{1,0:T(8,128)S(1)}, f32[130,1]{1,0:T(8,128)S(1)}, u32[]{:S(2)}, u32[]{:S(2)}) collective-permute-start(f32[130,1]{1,0:T(8,128)S(1)} %get-tuple-element.18), channel_id=1, source_target_pairs={{0,1},{1,2},{2,3},{4,5},{5,6},{6,7},{8,9},{9,10},{10,11},{12,13},{... | collective-permute-start | bytes 1568 | tf_op jit(solution)/shard_map/ppermute | solution.py:23
  78.7 5.2 %collective-permute-start.9 = (f32[130,1]{1,0:T(8,128)S(1)}, f32[130,1]{1,0:T(8,128)}, u32[]{:S(2)}, u32[]{:S(2)}) collective-permute-start(f32[130,1]{1,0:T(8,128)S(1)} %get-tuple-element.19), channel_id=1, source_target_pairs={{0,1},{1,2},{2,3},{4,5},{5,6},{6,7},{8,9},{9,10},{10,11},{12,13},{... | collective-permute-start | bytes 1568 | tf_op jit(solution)/shard_map/ppermute | solution.py:23
  83.9 12.6 %all-to-all-done = f32[4,1,131072]{2,1,0:T(1,128)S(1)} async-done(((f32[4,1,131072]{2,1,0:T(1,128)}), f32[4,1,131072]{2,1,0:T(1,128)S(1)}, u32[]{:S(2)}, u32[]{:S(2)}) %all-to-all-start) | async-done | bytes 2097184 | tf_op jit(solution)/shard_map/all_to_all | solution.py:97
  98.3 7.7 %reduce.8 = f32[4,131072]{1,0:T(4,128)S(1)} reduce(f32[4,1,131072]{2,1,0:T(1,128)} %copy-done.1, f32[]{:T(128)} %broadcast.270), dimensions={1}, to_apply=%all_to_all.17.reduce_sub_computation | reduce | bytes 4194308 | tf_op jit(solution)/shard_map/all_to_all | solution.py:97
  106.0 6.2 %reshape.265 = f32[2048,8,32]{2,1,0:T(8,128)} reshape(f32[4,131072]{1,0:T(4,128)S(1)} %reduce.8) | data formatting | bytes 4194304
  112.2 5.1 %copy.64 = f32[8,32,4,512]{3,1,2,0:T(8,128)S(1)} copy(f32[8,32,4,512]{1,0,3,2:T(8,128)} %bitcast.71) | data formatting | bytes 4194304 | tf_op jit(solution)/shard_map/all_to_all | solution.py:97
  117.3 5.2 %fusion.72 = (f32[1,4,32,512]{3,2,1,0:T(8,128)S(1)}, f32[1,4,32,512]{3,2,1,0:T(8,128)S(1)}) fusion(f32[8,4,32,512]{3,2,1,0:T(8,128)S(1)} %bitcast.73, f32[]{:T(128)} %bitcast.9, f32[]{:T(128)} %bitcast.8, f32[]{:T(128)} %bitcast.7, f32[]{:T(128)} %bitcast.6, f32[]{:T(128)} %bitcast.5, f32[]{:T(128)} %bitcast.4, f32[]{:T(128)} %bitcast.3, f32[]{:T(128)} %bitcast), kind=kLoop, calls=%fused_computation.165 | loop fusion | flops 983040 | bytes 2621472 | tf_op jit(solution)/shard_map/slice | solution.py:41
  123.9 3.7 %collective-permute-start.12 = (f32[1,512]{1,0:T(1,128)S(1)}, f32[1,512]{1,0:T(1,128)S(1)}, u32[]{:S(2)}, u32[]{:S(2)}) collective-permute-start(f32[1,512]{1,0:T(1,128)S(1)} %get-tuple-element.23), channel_id=1, source_target_pairs={{0,4},{4,8},{8,12},{12,16},{16,20},{20,24},{24,28},{1,5},{5,9},{9,... | collective-permute-start | bytes 6152 | tf_op jit(solution)/shard_map/ppermute | solution.py:23
  128.9 4.2 %collective-permute-done.13 = f32[1,512]{1,0:T(1,128)S(1)} collective-permute-done((f32[1,512]{1,0:T(1,128)S(1)}, f32[1,512]{1,0:T(1,128)S(1)}, u32[]{:S(2)}, u32[]{:S(2)}) %collective-permute-start.13) | collective-permute-done | bytes 2080 | tf_op jit(solution)/shard_map/ppermute | solution.py:24
  136.4 4.3 %collective-permute-done.15 = f32[130,1]{1,0:T(8,128)S(1)} collective-permute-done((f32[130,1]{1,0:T(8,128)S(1)}, f32[130,1]{1,0:T(8,128)S(1)}, u32[]{:S(2)}, u32[]{:S(2)}) %collective-permute-start.15) | collective-permute-done | bytes 552 | tf_op jit(solution)/shard_map/ppermute | solution.py:24
  145.6 11.8 %gather_fusion.1 = f32[2048]{0:T(1024)S(1)} fusion(f32[65536]{0:T(1024)S(1)} %bitcast.69, s32[2048]{0:T(1024)S(1)} %fusion.71), kind=kCustom, calls=%fused_computation.1 | custom fusion | bytes 24576 | tf_op jit(solution)/shard_map/gather | solution.py:107
  157.5 3.6 %collective-permute-start.18 = (f32[130,1]{1,0:T(8,128)S(1)}, f32[130,1]{1,0:T(8,128)S(1)}, u32[]{:S(2)}, u32[]{:S(2)}) collective-permute-start(f32[130,1]{1,0:T(8,128)S(1)} %get-tuple-element.13), channel_id=1, source_target_pairs={{0,1},{1,2},{2,3},{4,5},{5,6},{6,7},{8,9},{9,10},{10,11},{12,13},{... | collective-permute-start | bytes 1568 | tf_op jit(solution)/shard_map/ppermute | solution.py:23
  162.8 11.8 %gather_fusion.2 = f32[2048]{0:T(1024)S(1)} fusion(f32[65536]{0:T(1024)S(1)} %bitcast.67, s32[2048]{0:T(1024)S(1)} %fusion.71), kind=kCustom, calls=%fused_computation.2 | custom fusion | bytes 24576 | tf_op jit(solution)/shard_map/gather | solution.py:108
  175.2 11.8 %gather_fusion = f32[2048]{0:T(1024)S(1)} fusion(f32[65536]{0:T(1024)S(1)} %bitcast.68, s32[2048]{0:T(1024)S(1)} %fusion.71), kind=kCustom, calls=%fused_computation | custom fusion | bytes 24576 | tf_op jit(solution)/shard_map/gather | solution.py:107
  188.4 6.7 %scatter_custom_fusion = f32[3,6144]{0,1:T(8,128)S(1)} fusion(s32[2048]{0:T(1024)} %bitcast.85, f32[2048,3]{1,0:T(8,128)} %copy.67, f32[]{:T(128)} %constant.16.clone.1), kind=kCustom, calls=%fused_computation.35 | custom fusion | bytes 74240 | tf_op jit(solution)/shard_map/scatter | solution.py:113
  196.6 17.7 %all_to_all.24 = f32[3,32,192]{2,0,1:T(4,128)S(1)} all-to-all(f32[3,32,192]{2,0,1:T(4,128)S(1)} %copy.68), channel_id=1, replica_groups=mesh['gx'=8,'gy'=4] {'gx','gy'}, dimensions={1} | all-to-all | bytes 147456 | tf_op jit(solution)/shard_map/all_to_all | solution.py:114
  (104 shorter events, 43.7 us)
Async XLA Ops:
  3.5 7.3 %collective-permute-start = (f32[8,1,2048]{2,0,1:T(8,128)S(1)}, f32[8,1,2048]{2,0,1:T(8,128)S(1)}, u32[]{:S(2)}, u32[]{:S(2)}) collective-permute-start(f32[8,1,2048]{2,0,1:T(8,128)S(1)} %get-tuple-element.12), channel_id=1, source_target_pairs={{1,0},{2,1},{3,2},{4,3},{5,4},{6,5},{7,6},{8,7},{9,8},{10,9},{11,1... | collective-permute-start | bytes 196616 | tf_op jit(solution)/shard_map/ppermute | solution.py:24
  4.8 7.6 %collective-permute-start.1 = (f32[8,1,2048]{2,0,1:T(8,128)S(1)}, f32[8,1,2048]{2,0,1:T(8,128)S(1)}, u32[]{:S(2)}, u32[]{:S(2)}) collective-permute-start(f32[8,1,2048]{2,0,1:T(8,128)S(1)} %get-tuple-element.11), channel_id=1, source_target_pairs={{0,1},{1,2},{2,3},{3,4},{4,5},{5,6},{6,7},{7,8},{8,9},{9,10},{10,1... | collective-permute-start | bytes 196616 | tf_op jit(solution)/shard_map/ppermute | solution.py:23
  15.7 6.7 %collective-permute-start.2 = (f32[8,1,2048]{2,0,1:T(8,128)S(1)}, f32[8,1,2048]{2,0,1:T(8,128)S(1)}, u32[]{:S(2)}, u32[]{:S(2)}) collective-permute-start(f32[8,1,2048]{2,0,1:T(8,128)S(1)} %get-tuple-element.10), channel_id=1, source_target_pairs={{1,0},{2,1},{3,2},{4,3},{5,4},{6,5},{7,6},{8,7},{9,8},{10,9},{11,1... | collective-permute-start | bytes 196616 | tf_op jit(solution)/shard_map/ppermute | solution.py:24
  17.0 6.9 %collective-permute-start.3 = (f32[8,1,2048]{2,0,1:T(8,128)S(1)}, f32[8,1,2048]{2,0,1:T(8,128)S(1)}, u32[]{:S(2)}, u32[]{:S(2)}) collective-permute-start(f32[8,1,2048]{2,0,1:T(8,128)S(1)} %get-tuple-element.9), channel_id=1, source_target_pairs={{0,1},{1,2},{2,3},{3,4},{4,5},{5,6},{6,7},{7,8},{8,9},{9,10},{10,1... | collective-permute-start | bytes 196616 | tf_op jit(solution)/shard_map/ppermute | solution.py:23
  39.2 20.9 %copy-start.6 = (s32[2048,1]{0,1:T(1,128)S(1)}, s32[2048,1]{0,1:T(1,128)}, u32[]{:S(2)}) copy-start(s32[2048,1]{0,1:T(1,128)} %param.19) | copy-start | bytes 24580
  39.2 57.2 %all-to-all-start = ((f32[4,1,131072]{2,1,0:T(1,128)}), f32[4,1,131072]{2,1,0:T(1,128)S(1)}, u32[]{:S(2)}, u32[]{:S(2)}) async-start(f32[4,1,131072]{2,1,0:T(1,128)} %reshape.264), calls=%async_computation | async-start | bytes 4194304 | tf_op jit(solution)/shard_map/all_to_all | solution.py:97
  47.8 22.3 %copy-start.7 = (f32[8]{0:T(128)S(1)}, f32[8]{0:T(128)}, u32[]{:S(2)}) copy-start(f32[8]{0:T(128)} %param.15) | copy-start | bytes 100
  47.8 22.9 %collective-permute-start.4 = (f32[1,512]{1,0:T(1,128)S(1)}, f32[1,512]{1,0:T(1,128)S(1)}, u32[]{:S(2)}, u32[]{:S(2)}) collective-permute-start(f32[1,512]{1,0:T(1,128)S(1)} %get-tuple-element.26), channel_id=1, source_target_pairs={{0,4},{4,8},{8,12},{12,16},{16,20},{20,24},{24,28},{1,5},{5,9},{9,... | collective-permute-start | bytes 6152 | tf_op jit(solution)/shard_map/ppermute | solution.py:23
  52.3 18.5 %collective-permute-start.6 = (f32[1,512]{1,0:T(1,128)S(1)}, f32[1,512]{1,0:T(1,128)S(1)}, u32[]{:S(2)}, u32[]{:S(2)}) collective-permute-start(f32[1,512]{1,0:T(1,128)S(1)} %get-tuple-element.25), channel_id=1, source_target_pairs={{4,0},{8,4},{12,8},{16,12},{20,16},{24,20},{28,24},{5,1},{9,5},{13... | collective-permute-start | bytes 6152 | tf_op jit(solution)/shard_map/ppermute | solution.py:24
  53.6 23.1 %collective-permute-start.5 = (f32[1,512]{1,0:T(1,128)S(1)}, f32[1,512]{1,0:T(1,128)S(1)}, u32[]{:S(2)}, u32[]{:S(2)}) collective-permute-start(f32[1,512]{1,0:T(1,128)S(1)} %get-tuple-element.27), channel_id=1, source_target_pairs={{0,4},{4,8},{8,12},{12,16},{16,20},{20,24},{24,28},{1,5},{5,9},{9,... | collective-permute-start | bytes 6152 | tf_op jit(solution)/shard_map/ppermute | solution.py:23
  58.8 17.9 %collective-permute-start.7 = (f32[1,512]{1,0:T(1,128)S(1)}, f32[1,512]{1,0:T(1,128)S(1)}, u32[]{:S(2)}, u32[]{:S(2)}) collective-permute-start(f32[1,512]{1,0:T(1,128)S(1)} %get-tuple-element.28), channel_id=1, source_target_pairs={{4,0},{8,4},{12,8},{16,12},{20,16},{24,20},{28,24},{5,1},{9,5},{13... | collective-permute-start | bytes 6152 | tf_op jit(solution)/shard_map/ppermute | solution.py:24
  70.9 51.6 %collective-permute-start.10 = (f32[130,1]{1,0:T(8,128)S(1)}, f32[130,1]{1,0:T(8,128)S(1)}, u32[]{:S(2)}, u32[]{:S(2)}) collective-permute-start(f32[130,1]{1,0:T(8,128)S(1)} %get-tuple-element.17), channel_id=1, source_target_pairs={{1,0},{2,1},{3,2},{5,4},{6,5},{7,6},{9,8},{10,9},{11,10},{13,12},{... | collective-permute-start | bytes 1568 | tf_op jit(solution)/shard_map/ppermute | solution.py:24
  72.2 50.3 %collective-permute-start.8 = (f32[130,1]{1,0:T(8,128)S(1)}, f32[130,1]{1,0:T(8,128)S(1)}, u32[]{:S(2)}, u32[]{:S(2)}) collective-permute-start(f32[130,1]{1,0:T(8,128)S(1)} %get-tuple-element.18), channel_id=1, source_target_pairs={{0,1},{1,2},{2,3},{4,5},{5,6},{6,7},{8,9},{9,10},{10,11},{12,13},{... | collective-permute-start | bytes 1568 | tf_op jit(solution)/shard_map/ppermute | solution.py:23
  77.4 45.1 %collective-permute-start.11 = (f32[130,1]{1,0:T(8,128)}, f32[130,1]{1,0:T(8,128)}, u32[]{:S(2)}, u32[]{:S(2)}) collective-permute-start(f32[130,1]{1,0:T(8,128)} %get-tuple-element.20), channel_id=1, source_target_pairs={{1,0},{2,1},{3,2},{5,4},{6,5},{7,6},{9,8},{10,9},{11,10},{13,12},{... | collective-permute-start | bytes 1568 | tf_op jit(solution)/shard_map/ppermute | solution.py:24
  78.7 43.8 %collective-permute-start.9 = (f32[130,1]{1,0:T(8,128)S(1)}, f32[130,1]{1,0:T(8,128)}, u32[]{:S(2)}, u32[]{:S(2)}) collective-permute-start(f32[130,1]{1,0:T(8,128)S(1)} %get-tuple-element.19), channel_id=1, source_target_pairs={{0,1},{1,2},{2,3},{4,5},{5,6},{6,7},{8,9},{9,10},{10,11},{12,13},{... | collective-permute-start | bytes 1568 | tf_op jit(solution)/shard_map/ppermute | solution.py:23
  122.5 23.0 %copy-start.9 = (s32[2048]{0:T(1024)S(1)}, s32[2048]{0:T(1024)}, u32[]{:S(2)}) copy-start(s32[2048]{0:T(1024)} %param.18) | copy-start | bytes 24580
  123.9 5.0 %collective-permute-start.12 = (f32[1,512]{1,0:T(1,128)S(1)}, f32[1,512]{1,0:T(1,128)S(1)}, u32[]{:S(2)}, u32[]{:S(2)}) collective-permute-start(f32[1,512]{1,0:T(1,128)S(1)} %get-tuple-element.23), channel_id=1, source_target_pairs={{0,4},{4,8},{8,12},{12,16},{16,20},{20,24},{24,28},{1,5},{5,9},{9,... | collective-permute-start | bytes 6152 | tf_op jit(solution)/shard_map/ppermute | solution.py:23
  127.6 5.5 %collective-permute-start.13 = (f32[1,512]{1,0:T(1,128)S(1)}, f32[1,512]{1,0:T(1,128)S(1)}, u32[]{:S(2)}, u32[]{:S(2)}) collective-permute-start(f32[1,512]{1,0:T(1,128)S(1)} %get-tuple-element.24), channel_id=1, source_target_pairs={{4,0},{8,4},{12,8},{16,12},{20,16},{24,20},{28,24},{5,1},{9,5},{13... | collective-permute-start | bytes 6152 | tf_op jit(solution)/shard_map/ppermute | solution.py:24
  133.2 3.2 %collective-permute-start.14 = (f32[130,1]{1,0:T(8,128)S(1)}, f32[130,1]{1,0:T(8,128)S(1)}, u32[]{:S(2)}, u32[]{:S(2)}) collective-permute-start(f32[130,1]{1,0:T(8,128)S(1)} %get-tuple-element.15), channel_id=1, source_target_pairs={{0,1},{1,2},{2,3},{4,5},{5,6},{6,7},{8,9},{9,10},{10,11},{12,13},{... | collective-permute-start | bytes 1568 | tf_op jit(solution)/shard_map/ppermute | solution.py:23
  134.5 6.2 %collective-permute-start.15 = (f32[130,1]{1,0:T(8,128)S(1)}, f32[130,1]{1,0:T(8,128)S(1)}, u32[]{:S(2)}, u32[]{:S(2)}) collective-permute-start(f32[130,1]{1,0:T(8,128)S(1)} %get-tuple-element.16), channel_id=1, source_target_pairs={{1,0},{2,1},{3,2},{5,4},{6,5},{7,6},{9,8},{10,9},{11,10},{13,12},{... | collective-permute-start | bytes 1568 | tf_op jit(solution)/shard_map/ppermute | solution.py:24
  141.1 16.3 %collective-permute-start.16 = (f32[1,512]{1,0:T(1,128)S(1)}, f32[1,512]{1,0:T(1,128)S(1)}, u32[]{:S(2)}, u32[]{:S(2)}) collective-permute-start(f32[1,512]{1,0:T(1,128)S(1)} %get-tuple-element.21), channel_id=1, source_target_pairs={{0,4},{4,8},{8,12},{12,16},{16,20},{20,24},{24,28},{1,5},{5,9},{9,... | collective-permute-start | bytes 6152 | tf_op jit(solution)/shard_map/ppermute | solution.py:23
  144.2 13.2 %collective-permute-start.17 = (f32[1,512]{1,0:T(1,128)S(1)}, f32[1,512]{1,0:T(1,128)S(1)}, u32[]{:S(2)}, u32[]{:S(2)}) collective-permute-start(f32[1,512]{1,0:T(1,128)S(1)} %get-tuple-element.22), channel_id=1, source_target_pairs={{4,0},{8,4},{12,8},{16,12},{20,16},{24,20},{28,24},{5,1},{9,5},{13... | collective-permute-start | bytes 6152 | tf_op jit(solution)/shard_map/ppermute | solution.py:24
  157.5 17.1 %collective-permute-start.18 = (f32[130,1]{1,0:T(8,128)S(1)}, f32[130,1]{1,0:T(8,128)S(1)}, u32[]{:S(2)}, u32[]{:S(2)}) collective-permute-start(f32[130,1]{1,0:T(8,128)S(1)} %get-tuple-element.13), channel_id=1, source_target_pairs={{0,1},{1,2},{2,3},{4,5},{5,6},{6,7},{8,9},{9,10},{10,11},{12,13},{... | collective-permute-start | bytes 1568 | tf_op jit(solution)/shard_map/ppermute | solution.py:23
  161.2 13.5 %collective-permute-start.19 = (f32[130,1]{1,0:T(8,128)S(1)}, f32[130,1]{1,0:T(8,128)S(1)}, u32[]{:S(2)}, u32[]{:S(2)}) collective-permute-start(f32[130,1]{1,0:T(8,128)S(1)} %get-tuple-element.14), channel_id=1, source_target_pairs={{1,0},{2,1},{3,2},{5,4},{6,5},{7,6},{9,8},{10,9},{11,10},{13,12},{... | collective-permute-start | bytes 1568 | tf_op jit(solution)/shard_map/ppermute | solution.py:24
  (9 other events, 90.5 us)
where the time goes:
time: 218 us; the launch traced here: 217 us
  local copies, waits for them, and re-layouts  75 us (34%)
  starting transfers between devices  63.5 us (29%)
  other arithmetic  35.5 us (16%)
  waiting for transfers between devices  24.1 us (11%)
  blocking collectives  17.7 us (8%)
    ppermute x10, starting transfers between devices, with_halo(): before = lax.ppermute(last, axis, up)  41.7 us
    gather x2, local copies, waits for them, and re-layouts, body(): increment = warp.reshape(-1)[joint_cell] - warp_prev.reshape(-1)[joint_cell]  23.6 us
    all_to_all x1, blocking collectives, body(): lax.all_to_all(outgoing, ('gx', 'gy'), split_axis=1, concat_axis=1, tiled...  17.7 us
    unnamed x30, local copies, waits for them, and re-layouts  17.7 us
    ppermute x10, starting transfers between devices, with_halo(): after = lax.ppermute(leading, axis, down)  13.1 us
    all_to_all x1, waiting for transfers between devices, body(): lax.all_to_all(temp, 'gy', split_axis=2, concat_axis=1, tiled=True)  12.6 us
    gather x1, local copies, waits for them, and re-layouts, body(): theta = top.reshape(-1)[joint_cell]  11.8 us
    another operation x3, other arithmetic  9.41 us
  transfers between devices with their start and end apart: 21, of which 5 were waited for; matrix products, arithmetic and copies ran while one was open for 28% of the time, Pallas kernels for 0%

commit v1 on v0

--- a/solution.py
+++ b/solution.py
@@ -11,6 +11,22 @@
 sat_level = 2.5
 sat_power = 0.3
 harden = 2.0
+
+
+def pairwise_exchange(x, axis, split, join):
+    ways, here = (lax.axis_size(axis), lax.axis_index(axis))
+    width = x.shape[split] // ways
+    shape = list(x.shape)
+    shape[split] = width
+    height = shape[join]
+    shape[join] = height * ways
+    full = jnp.zeros(shape, x.dtype)
+    for mask in range(ways):
+        part = lax.dynamic_slice_in_dim(x, (here ^ mask) * width, width, axis=split)
+        if mask:
+            part = lax.ppermute(part, axis, [(d, d ^ mask) for d in range(ways)])
+        full = lax.dynamic_update_slice_in_dim(full, part, (here ^ mask) * height, axis=join)
+    return full
 
 
 def with_halo(array, sides, width):
@@ -94,7 +110,7 @@
     for step in range(STEPS):
         ext = with_halo(temp, ((("gx", "gy"), 1),), 1)
         temp = thermal_step(ext, heat_input, lateral, vertical)
-    relayed = lax.all_to_all(temp, "gy", split_axis=2, concat_axis=1, tiled=True)
+    relayed = pairwise_exchange(temp, "gy", 2, 1)
     load = moment_of(relayed, weighting)
     top = relayed[-1]
     e_pad = with_halo(modulus, (("gx", 0), ("gy", 1)), 1)

time: 218 us -> 211 us (0.968)
  local copies, waits for them, and re-layouts: 75 us -> 63.8 us
  waiting for transfers between devices: 24.1 us -> 34.8 us
  other arithmetic: 35.5 us -> 30.5 us
    ppermute x0 -> x3, waiting for transfers between devices: none -> 18.2 us  [pairwise_exchange(): part = lax.ppermute(part, axis, [(d, d ^ mask) for d in range(ways)])]
    unnamed x30 -> x40, local copies, waits for them, and re-layouts: 17.7 us -> 2 us
    all_to_all x1 -> x0, waiting for transfers between devices: 12.6 us -> none  [body(): lax.all_to_all(temp, 'gy', split_axis=2, concat_axis=1, tiled=True)]
    gather x2, local copies, waits for them, and re-layouts: 23.6 us -> 32.3 us  [body(): increment = warp.reshape(-1)[joint_cell] - warp_prev.reshape(-1)[joint_cell]]
    all_to_all x1 -> x0, starting transfers between devices: 8.62 us -> none  [body(): lax.all_to_all(temp, 'gy', split_axis=2, concat_axis=1, tiled=True)]
    all_to_all x1 -> x0, other arithmetic: 7.72 us -> none  [body(): lax.all_to_all(temp, 'gy', split_axis=2, concat_axis=1, tiled=True)]
    ppermute x10, waiting for transfers between devices: 8.46 us -> 14.9 us  [with_halo(): after = lax.ppermute(leading, axis, down)]
    ppermute x0 -> x3, starting transfers between devices: none -> 6.14 us  [pairwise_exchange(): part = lax.ppermute(part, axis, [(d, d ^ mask) for d in range(ways)])]
  transfers between devices with their start and end apart: 21 -> 23, of which waited for: 5 -> 7; matrix products, arithmetic and copies ran while one was open for 28% -> 28% of each run, Pallas kernels for 0% -> 0%
where the time goes in v1:
time: 211 us; the launch traced here: 210 us
  local copies, waits for them, and re-layouts  63.8 us (30%)
  starting transfers between devices  63.7 us (30%)
  waiting for transfers between devices  34.8 us (16%)
  other arithmetic  30.5 us (14%)
  blocking collectives  16.3 us (8%)
    ppermute x10, starting transfers between devices, with_halo(): before = lax.ppermute(last, axis, up)  44.5 us
    gather x2, local copies, waits for them, and re-layouts, body(): increment = warp.reshape(-1)[joint_cell] - warp_prev.reshape(-1)[joint_cell]  32.3 us
    ppermute x3, waiting for transfers between devices, pairwise_exchange(): part = lax.ppermute(part, axis, [(d, d ^ mask) for d in range(ways)])  18.2 us
    all_to_all x1, blocking collectives, body(): lax.all_to_all(outgoing, ('gx', 'gy'), split_axis=1, concat_axis=1, tiled...  16.3 us
    ppermute x10, waiting for transfers between devices, with_halo(): after = lax.ppermute(leading, axis, down)  14.9 us
    ppermute x10, starting transfers between devices, with_halo(): after = lax.ppermute(leading, axis, down)  13.1 us
    gather x1, local copies, waits for them, and re-layouts, body(): theta = top.reshape(-1)[joint_cell]  11.8 us
    another operation x3, other arithmetic  9.41 us
  transfers between devices with their start and end apart: 23, of which 7 were waited for; matrix products, arithmetic and copies ran while one was open for 28% of the time, Pallas kernels for 0%

profile of v1, /device:TPU:0, one launch (start us, length us, event | category | flops | bytes accessed | tf_op | source)
XLA Modules:
  0.0 210.5 jit_solution(10876824078558867096)
XLA Ops:
  3.2 5.6 %collective-permute-start.1 = (f32[8,1,2048]{2,1,0:T(1,128)S(1)}, f32[8,1,2048]{2,1,0:T(1,128)S(1)}, u32[]{:S(2)}, u32[]{:S(2)}) collective-permute-start(f32[8,1,2048]{2,1,0:T(1,128)S(1)} %get-tuple-element.15), channel_id=1, source_target_pairs={{0,1},{1,2},{2,3},{3,4},{4,5},{5,6},{6,7},{7,8},{8,9},{9,10},{10,1... | collective-permute-start | bytes 196616 | tf_op jit(solution)/shard_map/ppermute | solution.py:39
  9.6 4.0 %collective-permute-start.7 = (f32[1,512]{1,0:T(1,128)S(1)}, f32[1,512]{1,0:T(1,128)S(1)}, u32[]{:S(2)}, u32[]{:S(2)}) collective-permute-start(f32[1,512]{1,0:T(1,128)S(1)} %get-tuple-element.30), channel_id=1, source_target_pairs={{0,4},{4,8},{8,12},{12,16},{16,20},{20,24},{24,28},{1,5},{5,9},{9,... | collective-permute-start | bytes 6152 | tf_op jit(solution)/shard_map/ppermute | solution.py:39
  14.9 3.9 %subtract_multiply_fusion = f32[7,32,2048]{2,1,0:T(8,128)} fusion(f32[8,32,2048]{2,1,0:T(8,128)} %param.11, f32[7]{0:T(128)} %param.14), kind=kLoop, calls=%fused_computation.33 | loop fusion | flops 917504 | bytes 5505052 | tf_op jit(solution)/shard_map/mul | solution.py:49
  18.8 9.1 %reduce-window.6 = s32[32,16,128]{2,1,0:T(8,128)S(1)} reduce-window(s32[32,16,128]{2,1,0:T(8,128)S(1)} %fusion.61, s32[]{:T(128)} %constant.26.clone.1), window={size=1x1x128 pad=0_0x0_0x127_0}, to_apply=%region_0.1 | reduce-window | flops 8323072 | bytes 524292 | tf_op jit(solution)/shard_map/reduce-window
  30.8 1.9 fusion.11
  34.1 4.5 %collective-permute-start.3 = (f32[8,1,2048]{2,1,0:T(1,128)S(1)}, f32[8,1,2048]{2,1,0:T(1,128)S(1)}, u32[]{:S(2)}, u32[]{:S(2)}) collective-permute-start(f32[8,1,2048]{2,1,0:T(1,128)S(1)} %get-tuple-element.13), channel_id=1, source_target_pairs={{0,1},{1,2},{2,3},{3,4},{4,5},{5,6},{6,7},{7,8},{8,9},{9,10},{10,1... | collective-permute-start | bytes 196616 | tf_op jit(solution)/shard_map/ppermute | solution.py:39
  45.2 2.5 %collective-permute-start.4 = (f32[8,32,512]{2,1,0:T(8,128)}, f32[8,32,512]{2,1,0:T(8,128)}, u32[]{:S(2)}, u32[]{:S(2)}) collective-permute-start(f32[8,32,512]{2,1,0:T(8,128)} %get-tuple-element.11), channel_id=1, source_target_pairs={{0,1},{1,0},{2,3},{3,2},{4,5},{5,4},{6,7},{7,6},{8,9},{9,8},{10,11... | collective-permute-start | bytes 1572872 | tf_op jit(solution)/shard_map/ppermute | solution.py:27
  47.7 3.6 %collective-permute-start.5 = (f32[8,32,512]{2,1,0:T(8,128)}, f32[8,32,512]{2,1,0:T(8,128)}, u32[]{:S(2)}, u32[]{:S(2)}) collective-permute-start(f32[8,32,512]{2,1,0:T(8,128)} %get-tuple-element.10), channel_id=1, source_target_pairs={{0,2},{1,3},{2,0},{3,1},{4,6},{5,7},{6,4},{7,5},{8,10},{9,11},{10,... | collective-permute-start | bytes 1572872 | tf_op jit(solution)/shard_map/ppermute | solution.py:27
  53.5 5.7 %collective-permute-start.8 = (f32[1,512]{1,0:T(1,128)S(1)}, f32[1,512]{1,0:T(1,128)S(1)}, u32[]{:S(2)}, u32[]{:S(2)}) collective-permute-start(f32[1,512]{1,0:T(1,128)S(1)} %get-tuple-element.31), channel_id=1, source_target_pairs={{0,4},{4,8},{8,12},{12,16},{16,20},{20,24},{24,28},{1,5},{5,9},{9,... | collective-permute-start | bytes 6152 | tf_op jit(solution)/shard_map/ppermute | solution.py:39
  61.9 5.3 %collective-permute-done.4 = f32[8,32,512]{2,1,0:T(8,128)} collective-permute-done((f32[8,32,512]{2,1,0:T(8,128)}, f32[8,32,512]{2,1,0:T(8,128)}, u32[]{:S(2)}, u32[]{:S(2)}) %collective-permute-start.4) | collective-permute-done | bytes 524320 | tf_op jit(solution)/shard_map/ppermute | solution.py:27
  72.2 12.9 %collective-permute-done.6 = f32[8,32,512]{2,1,0:T(8,128)S(1)} collective-permute-done((f32[8,32,512]{2,1,0:T(8,128)}, f32[8,32,512]{2,1,0:T(8,128)S(1)}, u32[]{:S(2)}, u32[]{:S(2)}) %collective-permute-start.6) | collective-permute-done | bytes 524320 | tf_op jit(solution)/shard_map/ppermute | solution.py:27
  85.1 3.4 %collective-permute-done.14 = f32[130,1]{1,0:T(8,128)S(1)} collective-permute-done((f32[130,1]{1,0:T(8,128)S(1)}, f32[130,1]{1,0:T(8,128)S(1)}, u32[]{:S(2)}, u32[]{:S(2)}) %collective-permute-start.14) | collective-permute-done | bytes 552 | tf_op jit(solution)/shard_map/ppermute | solution.py:40
  88.6 5.4 %fusion.38 = (f32[128,512]{1,0:T(8,128)S(1)}, f32[128,512]{1,0:T(8,128)S(1)}) fusion(f32[130,1]{1,0:T(8,128)S(1)} %collective-permute-done.14, f32[1,512]{1,0:T(1,128)S(1)} %collective-permute-done.10, f32[128,512]{1,0:T(8,128)S(1)} %copy-done.4, f32[1,512]{1,0:T(1,128)S(1)} %collective-permute-done.8, f32[130,1]{1,0:T(8,128)S(1)} %collective-permute-done.12, ...), kind=kLoop, calls=%fused_computation.77 | loop fusion | flops 3407872 | bytes 3156032 | tf_op jit(solution)/shard_map/div | solution.py:75
  94.0 6.6 %collective-permute-start.15 = (f32[1,512]{1,0:T(1,128)S(1)}, f32[1,512]{1,0:T(1,128)S(1)}, u32[]{:S(2)}, u32[]{:S(2)}) collective-permute-start(f32[1,512]{1,0:T(1,128)S(1)} %get-tuple-element.27), channel_id=1, source_target_pairs={{0,4},{4,8},{8,12},{12,16},{16,20},{20,24},{24,28},{1,5},{5,9},{9,... | collective-permute-start | bytes 6152 | tf_op jit(solution)/shard_map/ppermute | solution.py:39
  101.9 7.1 %collective-permute-done.16 = f32[1,512]{1,0:T(1,128)S(1)} collective-permute-done((f32[1,512]{1,0:T(1,128)S(1)}, f32[1,512]{1,0:T(1,128)S(1)}, u32[]{:S(2)}, u32[]{:S(2)}) %collective-permute-start.16) | collective-permute-done | bytes 2080 | tf_op jit(solution)/shard_map/ppermute | solution.py:40
  109.1 9.5 %collective-permute-start.17 = (f32[130,1]{1,0:T(8,128)S(1)}, f32[130,1]{1,0:T(8,128)S(1)}, u32[]{:S(2)}, u32[]{:S(2)}) collective-permute-start(f32[130,1]{1,0:T(8,128)S(1)} %get-tuple-element.19), channel_id=1, source_target_pairs={{0,1},{1,2},{2,3},{4,5},{5,6},{6,7},{8,9},{9,10},{10,11},{12,13},{... | collective-permute-start | bytes 1568 | tf_op jit(solution)/shard_map/ppermute | solution.py:39
  120.5 4.3 %collective-permute-done.18 = f32[130,1]{1,0:T(8,128)S(1)} collective-permute-done((f32[130,1]{1,0:T(8,128)S(1)}, f32[130,1]{1,0:T(8,128)S(1)}, u32[]{:S(2)}, u32[]{:S(2)}) %collective-permute-start.18) | collective-permute-done | bytes 552 | tf_op jit(solution)/shard_map/ppermute | solution.py:40
  125.9 3.4 %collective-permute-start.19 = (f32[1,512]{1,0:T(1,128)}, f32[1,512]{1,0:T(1,128)}, u32[]{:S(2)}, u32[]{:S(2)}) collective-permute-start(f32[1,512]{1,0:T(1,128)} %get-tuple-element.25), channel_id=1, source_target_pairs={{0,4},{4,8},{8,12},{12,16},{16,20},{20,24},{24,28},{1,5},{5,9},{9,... | collective-permute-start | bytes 6152 | tf_op jit(solution)/shard_map/ppermute | solution.py:39
  130.7 20.6 %gather_fusion.1 = f32[2048]{0:T(1024)} fusion(f32[65536]{0:T(1024)S(1)} %bitcast.65, s32[2048]{0:T(1024)S(1)} %fusion.71), kind=kCustom, calls=%fused_computation.1 | custom fusion | bytes 24576 | tf_op jit(solution)/shard_map/gather | solution.py:123
  152.0 2.5 %collective-permute-start.21 = (f32[130,1]{1,0:T(8,128)S(1)}, f32[130,1]{1,0:T(8,128)S(1)}, u32[]{:S(2)}, u32[]{:S(2)}) collective-permute-start(f32[130,1]{1,0:T(8,128)S(1)} %get-tuple-element.17), channel_id=1, source_target_pairs={{0,1},{1,2},{2,3},{4,5},{5,6},{6,7},{8,9},{9,10},{10,11},{12,13},{... | collective-permute-start | bytes 1568 | tf_op jit(solution)/shard_map/ppermute | solution.py:39
  156.1 11.8 %gather_fusion.2 = f32[2048]{0:T(1024)S(1)} fusion(f32[65536]{0:T(1024)S(1)} %bitcast.63, s32[2048]{0:T(1024)S(1)} %fusion.71), kind=kCustom, calls=%fused_computation.2 | custom fusion | bytes 24576 | tf_op jit(solution)/shard_map/gather | solution.py:124
  170.1 11.8 %gather_fusion = f32[2048]{0:T(1024)S(1)} fusion(f32[65536]{0:T(1024)S(1)} %bitcast.64, s32[2048]{0:T(1024)S(1)} %fusion.71), kind=kCustom, calls=%fused_computation | custom fusion | bytes 24576 | tf_op jit(solution)/shard_map/gather | solution.py:123
  183.3 6.7 %scatter_custom_fusion = f32[3,6144]{0,1:T(8,128)S(1)} fusion(s32[2048]{0:T(1024)} %bitcast.77, f32[2048,3]{1,0:T(8,128)} %copy.20, f32[]{:T(128)} %constant.24.clone.1), kind=kCustom, calls=%fused_computation.34 | custom fusion | bytes 74240 | tf_op jit(solution)/shard_map/scatter | solution.py:129
  191.5 16.3 %all_to_all.9 = f32[3,32,192]{2,0,1:T(4,128)S(1)} all-to-all(f32[3,32,192]{2,0,1:T(4,128)S(1)} %copy.21), channel_id=1, replica_groups=mesh['gx'=8,'gy'=4] {'gx','gy'}, dimensions={1} | all-to-all | bytes 147456 | tf_op jit(solution)/shard_map/all_to_all | solution.py:130
  (118 shorter events, 41.0 us)
Async XLA Ops:
  1.9 26.7 %collective-permute-start = (f32[8,1,2048]{2,1,0:T(1,128)S(1)}, f32[8,1,2048]{2,1,0:T(1,128)S(1)}, u32[]{:S(2)}, u32[]{:S(2)}) collective-permute-start(f32[8,1,2048]{2,1,0:T(1,128)S(1)} %get-tuple-element.16), channel_id=1, source_target_pairs={{1,0},{2,1},{3,2},{4,3},{5,4},{6,5},{7,6},{8,7},{9,8},{10,9},{11,1... | collective-permute-start | bytes 196616 | tf_op jit(solution)/shard_map/ppermute | solution.py:40
  3.2 25.4 %collective-permute-start.1 = (f32[8,1,2048]{2,1,0:T(1,128)S(1)}, f32[8,1,2048]{2,1,0:T(1,128)S(1)}, u32[]{:S(2)}, u32[]{:S(2)}) collective-permute-start(f32[8,1,2048]{2,1,0:T(1,128)S(1)} %get-tuple-element.15), channel_id=1, source_target_pairs={{0,1},{1,2},{2,3},{3,4},{4,5},{5,6},{6,7},{7,8},{8,9},{9,10},{10,1... | collective-permute-start | bytes 196616 | tf_op jit(solution)/shard_map/ppermute | solution.py:39
  9.6 42.6 %collective-permute-start.7 = (f32[1,512]{1,0:T(1,128)S(1)}, f32[1,512]{1,0:T(1,128)S(1)}, u32[]{:S(2)}, u32[]{:S(2)}) collective-permute-start(f32[1,512]{1,0:T(1,128)S(1)} %get-tuple-element.30), channel_id=1, source_target_pairs={{0,4},{4,8},{8,12},{12,16},{16,20},{20,24},{24,28},{1,5},{5,9},{9,... | collective-permute-start | bytes 6152 | tf_op jit(solution)/shard_map/ppermute | solution.py:39
  13.6 39.8 %collective-permute-start.9 = (f32[1,512]{1,0:T(1,128)S(1)}, f32[1,512]{1,0:T(1,128)S(1)}, u32[]{:S(2)}, u32[]{:S(2)}) collective-permute-start(f32[1,512]{1,0:T(1,128)S(1)} %get-tuple-element.29), channel_id=1, source_target_pairs={{4,0},{8,4},{12,8},{16,12},{20,16},{24,20},{28,24},{5,1},{9,5},{13... | collective-permute-start | bytes 6152 | tf_op jit(solution)/shard_map/ppermute | solution.py:40
  32.8 6.3 %collective-permute-start.2 = (f32[8,1,2048]{2,1,0:T(1,128)S(1)}, f32[8,1,2048]{2,1,0:T(1,128)S(1)}, u32[]{:S(2)}, u32[]{:S(2)}) collective-permute-start(f32[8,1,2048]{2,1,0:T(1,128)S(1)} %get-tuple-element.14), channel_id=1, source_target_pairs={{1,0},{2,1},{3,2},{4,3},{5,4},{6,5},{7,6},{8,7},{9,8},{10,9},{11,1... | collective-permute-start | bytes 196616 | tf_op jit(solution)/shard_map/ppermute | solution.py:40
  34.1 6.7 %collective-permute-start.3 = (f32[8,1,2048]{2,1,0:T(1,128)S(1)}, f32[8,1,2048]{2,1,0:T(1,128)S(1)}, u32[]{:S(2)}, u32[]{:S(2)}) collective-permute-start(f32[8,1,2048]{2,1,0:T(1,128)S(1)} %get-tuple-element.13), channel_id=1, source_target_pairs={{0,1},{1,2},{2,3},{3,4},{4,5},{5,6},{6,7},{7,8},{8,9},{9,10},{10,1... | collective-permute-start | bytes 196616 | tf_op jit(solution)/shard_map/ppermute | solution.py:39
  45.2 22.0 %collective-permute-start.4 = (f32[8,32,512]{2,1,0:T(8,128)}, f32[8,32,512]{2,1,0:T(8,128)}, u32[]{:S(2)}, u32[]{:S(2)}) collective-permute-start(f32[8,32,512]{2,1,0:T(8,128)} %get-tuple-element.11), channel_id=1, source_target_pairs={{0,1},{1,0},{2,3},{3,2},{4,5},{5,4},{6,7},{7,6},{8,9},{9,8},{10,11... | collective-permute-start | bytes 1572872 | tf_op jit(solution)/shard_map/ppermute | solution.py:27
  47.7 22.1 %collective-permute-start.5 = (f32[8,32,512]{2,1,0:T(8,128)}, f32[8,32,512]{2,1,0:T(8,128)}, u32[]{:S(2)}, u32[]{:S(2)}) collective-permute-start(f32[8,32,512]{2,1,0:T(8,128)} %get-tuple-element.10), channel_id=1, source_target_pairs={{0,2},{1,3},{2,0},{3,1},{4,6},{5,7},{6,4},{7,5},{8,10},{9,11},{10,... | collective-permute-start | bytes 1572872 | tf_op jit(solution)/shard_map/ppermute | solution.py:27
  51.4 33.7 %collective-permute-start.6 = (f32[8,32,512]{2,1,0:T(8,128)}, f32[8,32,512]{2,1,0:T(8,128)S(1)}, u32[]{:S(2)}, u32[]{:S(2)}) collective-permute-start(f32[8,32,512]{2,1,0:T(8,128)} %get-tuple-element.9), channel_id=1, source_target_pairs={{0,3},{1,2},{2,1},{3,0},{4,7},{5,6},{6,5},{7,4},{8,11},{9,10},{10,... | collective-permute-start | bytes 1572872 | tf_op jit(solution)/shard_map/ppermute | solution.py:27
  52.1 72.7 %copy-start.9 = (f32[1,512]{1,0:T(1,128)}, f32[1,512]{1,0:T(1,128)S(1)}, u32[]{:S(2)}) copy-start(f32[1,512]{1,0:T(1,128)S(1)} %collective-permute-done.7) | copy-start | bytes 6148
  52.1 7.1 %collective-permute-start.10 = (f32[1,512]{1,0:T(1,128)S(1)}, f32[1,512]{1,0:T(1,128)S(1)}, u32[]{:S(2)}, u32[]{:S(2)}) collective-permute-start(f32[1,512]{1,0:T(1,128)S(1)} %get-tuple-element.32), channel_id=1, source_target_pairs={{4,0},{8,4},{12,8},{16,12},{20,16},{24,20},{28,24},{5,1},{9,5},{13... | collective-permute-start | bytes 6152 | tf_op jit(solution)/shard_map/ppermute | solution.py:40
  53.5 7.1 %collective-permute-start.8 = (f32[1,512]{1,0:T(1,128)S(1)}, f32[1,512]{1,0:T(1,128)S(1)}, u32[]{:S(2)}, u32[]{:S(2)}) collective-permute-start(f32[1,512]{1,0:T(1,128)S(1)} %get-tuple-element.31), channel_id=1, source_target_pairs={{0,4},{4,8},{8,12},{12,16},{16,20},{20,24},{24,28},{1,5},{5,9},{9,... | collective-permute-start | bytes 6152 | tf_op jit(solution)/shard_map/ppermute | solution.py:39
  59.2 25.9 %collective-permute-start.11 = (f32[130,1]{1,0:T(8,128)S(1)}, f32[130,1]{1,0:T(8,128)S(1)}, u32[]{:S(2)}, u32[]{:S(2)}) collective-permute-start(f32[130,1]{1,0:T(8,128)S(1)} %get-tuple-element.22), channel_id=1, source_target_pairs={{0,1},{1,2},{2,3},{4,5},{5,6},{6,7},{8,9},{9,10},{10,11},{12,13},{... | collective-permute-start | bytes 1568 | tf_op jit(solution)/shard_map/ppermute | solution.py:39
  60.5 24.6 %collective-permute-start.13 = (f32[130,1]{1,0:T(8,128)S(1)}, f32[130,1]{1,0:T(8,128)S(1)}, u32[]{:S(2)}, u32[]{:S(2)}) collective-permute-start(f32[130,1]{1,0:T(8,128)S(1)} %get-tuple-element.21), channel_id=1, source_target_pairs={{1,0},{2,1},{3,2},{5,4},{6,5},{7,6},{9,8},{10,9},{11,10},{13,12},{... | collective-permute-start | bytes 1568 | tf_op jit(solution)/shard_map/ppermute | solution.py:40
  67.2 17.9 %collective-permute-start.12 = (f32[130,1]{1,0:T(8,128)S(1)}, f32[130,1]{1,0:T(8,128)S(1)}, u32[]{:S(2)}, u32[]{:S(2)}) collective-permute-start(f32[130,1]{1,0:T(8,128)S(1)} %get-tuple-element.23), channel_id=1, source_target_pairs={{0,1},{1,2},{2,3},{4,5},{5,6},{6,7},{8,9},{9,10},{10,11},{12,13},{... | collective-permute-start | bytes 1568 | tf_op jit(solution)/shard_map/ppermute | solution.py:39
  69.8 18.8 %collective-permute-start.14 = (f32[130,1]{1,0:T(8,128)S(1)}, f32[130,1]{1,0:T(8,128)S(1)}, u32[]{:S(2)}, u32[]{:S(2)}) collective-permute-start(f32[130,1]{1,0:T(8,128)S(1)} %get-tuple-element.24), channel_id=1, source_target_pairs={{1,0},{2,1},{3,2},{5,4},{6,5},{7,6},{9,8},{10,9},{11,10},{13,12},{... | collective-permute-start | bytes 1568 | tf_op jit(solution)/shard_map/ppermute | solution.py:40
  94.0 7.9 %collective-permute-start.15 = (f32[1,512]{1,0:T(1,128)S(1)}, f32[1,512]{1,0:T(1,128)S(1)}, u32[]{:S(2)}, u32[]{:S(2)}) collective-permute-start(f32[1,512]{1,0:T(1,128)S(1)} %get-tuple-element.27), channel_id=1, source_target_pairs={{0,4},{4,8},{8,12},{12,16},{16,20},{20,24},{24,28},{1,5},{5,9},{9,... | collective-permute-start | bytes 6152 | tf_op jit(solution)/shard_map/ppermute | solution.py:39
  100.6 8.4 %collective-permute-start.16 = (f32[1,512]{1,0:T(1,128)S(1)}, f32[1,512]{1,0:T(1,128)S(1)}, u32[]{:S(2)}, u32[]{:S(2)}) collective-permute-start(f32[1,512]{1,0:T(1,128)S(1)} %get-tuple-element.28), channel_id=1, source_target_pairs={{4,0},{8,4},{12,8},{16,12},{20,16},{24,20},{28,24},{5,1},{9,5},{13... | collective-permute-start | bytes 6152 | tf_op jit(solution)/shard_map/ppermute | solution.py:40
  109.1 11.4 %collective-permute-start.17 = (f32[130,1]{1,0:T(8,128)S(1)}, f32[130,1]{1,0:T(8,128)S(1)}, u32[]{:S(2)}, u32[]{:S(2)}) collective-permute-start(f32[130,1]{1,0:T(8,128)S(1)} %get-tuple-element.19), channel_id=1, source_target_pairs={{0,1},{1,2},{2,3},{4,5},{5,6},{6,7},{8,9},{9,10},{10,11},{12,13},{... | collective-permute-start | bytes 1568 | tf_op jit(solution)/shard_map/ppermute | solution.py:39
  118.6 6.2 %collective-permute-start.18 = (f32[130,1]{1,0:T(8,128)S(1)}, f32[130,1]{1,0:T(8,128)S(1)}, u32[]{:S(2)}, u32[]{:S(2)}) collective-permute-start(f32[130,1]{1,0:T(8,128)S(1)} %get-tuple-element.20), channel_id=1, source_target_pairs={{1,0},{2,1},{3,2},{5,4},{6,5},{7,6},{9,8},{10,9},{11,10},{13,12},{... | collective-permute-start | bytes 1568 | tf_op jit(solution)/shard_map/ppermute | solution.py:40
  125.9 25.4 %collective-permute-start.19 = (f32[1,512]{1,0:T(1,128)}, f32[1,512]{1,0:T(1,128)}, u32[]{:S(2)}, u32[]{:S(2)}) collective-permute-start(f32[1,512]{1,0:T(1,128)} %get-tuple-element.25), channel_id=1, source_target_pairs={{0,4},{4,8},{8,12},{12,16},{16,20},{20,24},{24,28},{1,5},{5,9},{9,... | collective-permute-start | bytes 6152 | tf_op jit(solution)/shard_map/ppermute | solution.py:39
  129.3 22.0 %collective-permute-start.20 = (f32[1,512]{1,0:T(1,128)}, f32[1,512]{1,0:T(1,128)}, u32[]{:S(2)}, u32[]{:S(2)}) collective-permute-start(f32[1,512]{1,0:T(1,128)} %get-tuple-element.26), channel_id=1, source_target_pairs={{4,0},{8,4},{12,8},{16,12},{20,16},{24,20},{28,24},{5,1},{9,5},{13... | collective-permute-start | bytes 6152 | tf_op jit(solution)/shard_map/ppermute | solution.py:40
  152.0 15.9 %collective-permute-start.21 = (f32[130,1]{1,0:T(8,128)S(1)}, f32[130,1]{1,0:T(8,128)S(1)}, u32[]{:S(2)}, u32[]{:S(2)}) collective-permute-start(f32[130,1]{1,0:T(8,128)S(1)} %get-tuple-element.17), channel_id=1, source_target_pairs={{0,1},{1,2},{2,3},{4,5},{5,6},{6,7},{8,9},{9,10},{10,11},{12,13},{... | collective-permute-start | bytes 1568 | tf_op jit(solution)/shard_map/ppermute | solution.py:39
  154.5 13.4 %collective-permute-start.22 = (f32[130,1]{1,0:T(8,128)S(1)}, f32[130,1]{1,0:T(8,128)}, u32[]{:S(2)}, u32[]{:S(2)}) collective-permute-start(f32[130,1]{1,0:T(8,128)S(1)} %get-tuple-element.18), channel_id=1, source_target_pairs={{1,0},{2,1},{3,2},{5,4},{6,5},{7,6},{9,8},{10,9},{11,10},{13,12},{... | collective-permute-start | bytes 1568 | tf_op jit(solution)/shard_map/ppermute | solution.py:40
  (17 other events, 241.8 us)
